TPU v7x, 32 devices: a whole 2x2x4 slice. The times are simulated.
32 devices in a mesh: tile: 8 (over y, x, core), slab: 4 (over z).
Axes of the slice: x: 2, y: 2, z: 4, core: 2. Of those that a mesh axis runs over, the one named last changes fastest.
Arguments:
- estimate: float32 [64, 128, 512], P('slab', 'tile'), may hold values from 0.5 to 2
- observed: float32 [64, 128, 512], P('slab', 'tile'), may hold values from 0.25 to 4
- kernel_rows: float32 [31], replicated, may hold values from 0.001 to 1
- kernel_columns: float32 [31], replicated, may hold values from 0.001 to 1
- kernel_planes: float32 [31], replicated, may hold values from 0.001 to 1
Outputs:
- new_estimate: float32 [64, 128, 512], P('slab', 'tile')
- pyramid_level: float32 [64, 64, 256], P('slab', 'tile')
All inputs are finite; a program needn't handle non-finite values.
Results may differ from a plain program's by a relative error of at most 0.00005.
Values sent between devices are 32-bit elements; how exact they have to be, the bound alone decides.
No kernel may reach another device: no remote copies, remote signals or barrier semaphores. Data moves between devices by JAX's collectives and lax.ppermute only.
A program may use at most 64 MiB of HBM per device.

v0:
```python
import jax
import jax.numpy as jnp
from jax import lax
from jax.sharding import PartitionSpec as P

PRECISE = lax.Precision.HIGHEST


def extended(shard, sides, width):
    for axis, dim in sides:
        devices, length = (lax.axis_size(axis), shard.shape[dim])
        up = [(i, (i + 1) % devices) for i in range(devices - 1)]
        down = [(j, i) for i, j in up]
        last = lax.slice_in_dim(shard, length - width, length, axis=dim)
        initial = lax.slice_in_dim(shard, 0, width, axis=dim)
        before = lax.ppermute(last, axis, up)
        after = lax.ppermute(initial, axis, down)
        shard = jnp.concatenate([before, shard, after], axis=dim)
    return shard


def banded(kernel, row_count, col_count, orient, anchor):
    tap_count = kernel.shape[0]
    offset_index = (
        orient
        * (
            lax.broadcasted_iota(jnp.int32, (row_count, col_count), 0)
            - lax.broadcasted_iota(jnp.int32, (row_count, col_count), 1)
        )
        + anchor
    )
    inside = (offset_index >= 0) & (offset_index < tap_count)
    values = jnp.take(kernel, jnp.clip(offset_index, 0, tap_count - 1))
    return jnp.where(inside, values, jnp.zeros_like(values))


def pyramid_matrix(row_count, col_count, anchor):
    offset_index = (
        lax.broadcasted_iota(jnp.int32, (row_count, col_count), 0)
        - 2 * lax.broadcasted_iota(jnp.int32, (row_count, col_count), 1)
        + anchor
    )
    outer = (offset_index == 0) | (offset_index == 3)
    middle = (offset_index == 1) | (offset_index == 2)
    return jnp.where(
        outer, jnp.float32(0.125), jnp.where(middle, jnp.float32(0.375), jnp.float32(0.0))
    )


def across_depth(volume, matrix):
    return jnp.einsum("pxy,pq->qxy", volume, matrix, precision=PRECISE)


def across_rows(volume, matrix):
    return jnp.einsum("zpy,pq->zqy", volume, matrix, precision=PRECISE)


def across_columns(volume, matrix):
    return jnp.dot(volume, matrix, precision=PRECISE)


def shards(estimate, observed, kernel_rows, kernel_columns, kernel_planes):
    plane_count, row_count, col_count = estimate.shape
    reach_cells = (kernel_rows.shape[0] - 1) // 2
    groups = lax.axis_size("slab")
    planes_all = plane_count * groups
    padded = extended(estimate, (("tile", 1),), reach_cells)
    partial_value = across_rows(
        padded, banded(kernel_rows, row_count + 2 * reach_cells, row_count, 1, 0)
    )
    partial_value = across_columns(
        partial_value, banded(kernel_columns, col_count, col_count, 1, reach_cells)
    )
    forward_depth = banded(kernel_planes, planes_all, planes_all, 1, reach_cells)
    backward_depth = banded(kernel_planes, planes_all, planes_all, -1, reach_cells)
    turned = across_depth(
        lax.all_to_all(partial_value, "slab", split_axis=2, concat_axis=0, tiled=True),
        forward_depth,
    )
    blurred = lax.all_to_all(turned, "slab", split_axis=0, concat_axis=2, tiled=True)
    quotient = observed / blurred
    turned_back = across_depth(
        lax.all_to_all(quotient, "slab", split_axis=2, concat_axis=0, tiled=True), backward_depth
    )
    back_field = lax.all_to_all(turned_back, "slab", split_axis=0, concat_axis=2, tiled=True)
    spread = across_columns(
        back_field, banded(kernel_columns, col_count, col_count, -1, reach_cells)
    )
    padded_spread = extended(spread, (("tile", 1),), reach_cells)
    correction = across_rows(
        padded_spread,
        banded(kernel_rows, row_count + 2 * reach_cells, row_count, -1, 2 * reach_cells),
    )
    new_estimate = estimate * correction
    halved = across_columns(new_estimate, pyramid_matrix(col_count, col_count // 2, 1))
    padded_halved = extended(halved, (("tile", 1),), 1)
    pyramid_level = across_rows(padded_halved, pyramid_matrix(row_count + 2, row_count // 2, 0))
    return (new_estimate, pyramid_level)


def solution(mesh):
    in_specs = (P("slab", "tile", None), P("slab", "tile", None), P(), P(), P())
    out_specs = (P("slab", "tile", None), P("slab", "tile", None))
    return jax.shard_map(shards, mesh=mesh, in_specs=in_specs, out_specs=out_specs, check_vma=False)
```

profile of v0, /device:TPU:1, one launch (start us, length us, event | category | flops | bytes accessed | tf_op | source)
XLA Modules:
  0.0 230.6 jit_solution(3255726964246776414)
XLA Ops:
  0.6 0.0 copy-start
  0.7 1.3 fusion.571
  2.0 4.5 %collective-permute-start = (f32[16,15,512]{2,1,0:T(8,128)S(1)}, f32[16,15,512]{2,1,0:T(8,128)S(1)}, u32[]{:S(2)}, u32[]{:S(2)}) collective-permute-start(f32[16,15,512]{2,1,0:T(8,128)S(1)} %get-tuple-element.7), channel_id=1, source_target_pairs={{0,4},{4,8},{8,12},{12,16},{16,20},{20,24},{24,28},{1,5},{5,9},{9,... | collective-permute-start | bytes 1474568 | tf_op jit(solution)/shard_map/ppermute | solution.py:16
  6.5 1.9 collective-permute-start.1
  8.5 0.1 reshape.155
  8.6 0.0 copy-start.5
  8.6 0.0 copy-start.2
  8.6 4.8 %gather_fusion.3 = f32[736]{0:T(1024)S(1)} fusion(f32[31]{0:T(128)S(1)} %copy-done.1, s32[1024]{0:T(1024)S(1)} %pad_clamp_fusion), kind=kCustom, calls=%fused_computation.2.clone | custom fusion | bytes 8832 | tf_op jit(solution)/shard_map/jit(_take)/gather | solution.py:33
  13.4 0.1 reshape.158
  13.5 0.7 fusion.574
  14.2 0.7 fusion.573
  14.9 0.0 collective-permute-done
  14.9 5.0 %collective-permute-done.1 = f32[16,15,512]{2,1,0:T(8,128)S(1)} collective-permute-done((f32[16,15,512]{2,1,0:T(8,128)S(1)}, f32[16,15,512]{2,1,0:T(8,128)S(1)}, u32[]{:S(2)}, u32[]{:S(2)}) %collective-permute-start.1) | collective-permute-done | bytes 491552 | tf_op jit(solution)/shard_map/ppermute | solution.py:17
  19.9 1.0 fusion.15
  20.9 23.0 %fusion.23 = f32[16,16,512]{2,1,0:T(8,128)S(1)} fusion(f32[16,16,512]{2,1,0:T(8,128)S(1)} %fusion.15, f32[]{:T(128)} %bitcast.35, f32[]{:T(128)} %bitcast.34, f32[]{:T(128)} %bitcast.33, f32[]{:T(128)} %bitcast.32, f32[]{:T(128)} %bitcast.31, f32[]{:T(128)} %bitcast.30, f32[]{:T(128)} %bitcast.29, f32[]{:T(128)} %bitcast.28, f32[]{:T(128)} %bitcast.27, ...), kind=kOutput, calls=%fused_computation.25 | convolution fusion | flops 824705024 | bytes 1048700 | tf_op jit(solution)/shard_map/dot_general | solution.py:59
  43.9 3.6 %copy.19 = f32[16,16,512]{1,0,2:T(8,128)} copy(f32[16,16,512]{2,1,0:T(8,128)S(1)} %fusion.23) | data formatting | bytes 1048576 | tf_op jit(solution)/shard_map/dot_general | solution.py:59
  47.5 4.6 %reshape.229 = f32[4,1,32768]{2,1,0:T(1,128)} reshape(f32[512,16,16]{2,1,0:T(8,128)} %bitcast.121) | data formatting | bytes 1048576
  52.1 4.6 %all-to-all-start = ((f32[4,1,32768]{2,1,0:T(1,128)}), f32[4,1,32768]{2,1,0:T(1,128)S(1)}, u32[]{:S(2)}, u32[]{:S(2)}) async-start(f32[4,1,32768]{2,1,0:T(1,128)} %reshape.229), calls=%async_computation | async-start | bytes 1048576 | tf_op jit(solution)/shard_map/all_to_all | solution.py:77
  56.7 0.1 reshape.151
  56.8 24.7 %gather_fusion.2 = f32[4096]{0:T(1024)S(1)} fusion(f32[31]{0:T(128)S(1)} %copy-done, s32[4096]{0:T(1024)S(1)} %broadcast_clamp_fusion), kind=kCustom, calls=%fused_computation.3.clone | custom fusion | bytes 49152 | tf_op jit(solution)/shard_map/jit(_take)/gather | solution.py:33
  81.5 0.1 reshape.154
  81.6 0.0 all-to-all-done
  81.6 0.5 broadcast.948
  82.1 2.1 reduce
  84.2 3.4 %reshape.230 = f32[512,16,16]{2,1,0:T(8,128)} reshape(f32[4,32768]{1,0:T(4,128)S(1)} %reduce) | data formatting | bytes 1048576
  87.7 3.3 %copy.20 = f32[16,16,4,128]{3,0,2,1:T(8,128)S(1)} copy(f32[16,16,4,128]{1,0,3,2:T(8,128)} %bitcast.122) | data formatting | bytes 1048576 | tf_op jit(solution)/shard_map/all_to_all | solution.py:77
  91.0 0.0 copy-start.3
  91.0 0.6 fusion.379
  91.7 1.1 copy.22
  92.8 4.5 %all-to-all-start.1 = ((f32[64,16,128]{2,1,0:T(8,128)}), f32[64,16,128]{2,1,0:T(8,128)S(1)}, u32[]{:S(2)}, u32[]{:S(2)}) async-start(f32[64,16,128]{2,1,0:T(8,128)} %copy.22), calls=%async_computation.1 | async-start | bytes 1048576 | tf_op jit(solution)/shard_map/all_to_all | solution.py:80
  97.3 3.7 %copy.24 = f32[16,16,512]{1,0,2:T(8,128)} copy(f32[16,16,512]{2,1,0:T(8,128)S(1)} %copy-done.3) | data formatting | bytes 1048576 | tf_op args[1]
  100.9 5.6 %all-to-all-done.1 = f32[64,16,128]{2,1,0:T(8,128)S(1)} async-done(((f32[64,16,128]{2,1,0:T(8,128)}), f32[64,16,128]{2,1,0:T(8,128)S(1)}, u32[]{:S(2)}, u32[]{:S(2)}) %all-to-all-start.1) | async-done | bytes 524320 | tf_op jit(solution)/shard_map/all_to_all | solution.py:80
  106.5 2.8 %copy.23 = f32[16,16,4,128]{1,0,3,2:T(8,128)} copy(f32[16,16,4,128]{3,1,0,2:T(8,128)S(1)} %bitcast.124) | data formatting | bytes 1048576 | tf_op jit(solution)/shard_map/all_to_all | solution.py:80
  109.3 6.0 %bitcast_divide_fusion = f32[16,16,512]{1,0,2:T(8,128)} fusion(f32[16,16,512]{1,0,2:T(8,128)} %copy.24, f32[16,16,4,128]{1,0,3,2:T(8,128)} %copy.23), kind=kLoop, calls=%fused_computation.4 | loop fusion | flops 131072 | bytes 1572864 | tf_op jit(solution)/shard_map/div | solution.py:81
  115.3 4.6 %reshape.231 = f32[4,1,32768]{2,1,0:T(1,128)} reshape(f32[512,16,16]{2,1,0:T(8,128)} %bitcast.120) | data formatting | bytes 1048576
  119.9 3.5 %all-to-all-start.2 = ((f32[4,1,32768]{2,1,0:T(1,128)}), f32[4,1,32768]{2,1,0:T(1,128)S(1)}, u32[]{:S(2)}, u32[]{:S(2)}) async-start(f32[4,1,32768]{2,1,0:T(1,128)} %reshape.231), calls=%async_computation.2 | async-start | bytes 1048576 | tf_op jit(solution)/shard_map/all_to_all | solution.py:83
  123.5 0.1 reshape.147
  123.5 24.7 %gather_fusion.1 = f32[4096]{0:T(1024)S(1)} fusion(f32[31]{0:T(128)S(1)} %copy-done, s32[4096]{0:T(1024)S(1)} %broadcast_clamp_fusion.1), kind=kCustom, calls=%fused_computation.1.clone | custom fusion | bytes 49152 | tf_op jit(solution)/shard_map/jit(_take)/gather | solution.py:33
  148.2 0.1 reshape.150
  148.3 0.0 all-to-all-done.2
  148.3 2.1 reduce.1
  150.4 3.4 %reshape.232 = f32[512,16,16]{2,1,0:T(8,128)} reshape(f32[4,32768]{1,0:T(4,128)S(1)} %reduce.1) | data formatting | bytes 1048576
  153.8 3.3 %copy.25 = f32[16,16,4,128]{3,0,2,1:T(8,128)S(1)} copy(f32[16,16,4,128]{1,0,3,2:T(8,128)} %bitcast.123) | data formatting | bytes 1048576 | tf_op jit(solution)/shard_map/all_to_all | solution.py:83
  157.2 0.6 fusion.381
  157.8 0.3 copy.27
  158.1 15.2 %all_to_all.72 = f32[64,16,128]{2,1,0:T(8,128)S(1)} all-to-all(f32[64,16,128]{2,1,0:T(8,128)S(1)} %copy.27), channel_id=1, replica_groups=mesh['tile'=8,'slab'=4] {'slab'}, dimensions={0} | all-to-all | bytes 1048576 | tf_op jit(solution)/shard_map/all_to_all | solution.py:85
  173.4 0.3 copy.39
  173.7 0.2 all_to_all.67
  174.0 22.9 %fusion.21 = f32[16,16,512]{2,1,0:T(8,128)S(1)} fusion(f32[16,16,512]{2,1,0:T(8,128)S(1)} %all_to_all.67, f32[]{:T(128)} %bitcast.35, f32[]{:T(128)} %bitcast.34, f32[]{:T(128)} %bitcast.33, f32[]{:T(128)} %bitcast.32, f32[]{:T(128)} %bitcast.31, f32[]{:T(128)} %bitcast.30, f32[]{:T(128)} %bitcast.29, f32[]{:T(128)} %bitcast.28, f32[]{:T(128)} %bitcast.27, ...), kind=kOutput, calls=%fused_computation.23 | convolution fusion | flops 824967168 | bytes 1048700 | tf_op jit(solution)/shard_map/dot_general | solution.py:59
  196.9 0.1 fusion.570
  197.0 13.3 %collective-permute-start.2 = (f32[16,15,512]{2,1,0:T(8,128)S(1)}, f32[16,15,512]{2,1,0:T(8,128)S(1)}, u32[]{:S(2)}, u32[]{:S(2)}) collective-permute-start(f32[16,15,512]{2,1,0:T(8,128)S(1)} %get-tuple-element.4), channel_id=1, source_target_pairs={{0,4},{4,8},{8,12},{12,16},{16,20},{20,24},{24,28},{1,5},{5,9},{9,... | collective-permute-start | bytes 1474568 | tf_op jit(solution)/shard_map/ppermute | solution.py:16
  210.3 2.1 collective-permute-start.3
  212.5 0.1 reshape.143
  212.5 4.8 %gather_fusion = f32[736]{0:T(1024)S(1)} fusion(f32[31]{0:T(128)S(1)} %copy-done.1, s32[1024]{0:T(1024)S(1)} %pad_clamp_fusion.1), kind=kCustom, calls=%fused_computation.clone | custom fusion | bytes 8832 | tf_op jit(solution)/shard_map/jit(_take)/gather | solution.py:33
  217.3 0.1 reshape.146
  217.4 0.0 collective-permute-done.2
  217.4 3.4 %collective-permute-done.3 = f32[16,15,512]{2,1,0:T(8,128)S(1)} collective-permute-done((f32[16,15,512]{2,1,0:T(8,128)S(1)}, f32[16,15,512]{2,1,0:T(8,128)S(1)}, u32[]{:S(2)}, u32[]{:S(2)}) %collective-permute-start.3) | collective-permute-done | bytes 491552 | tf_op jit(solution)/shard_map/ppermute | solution.py:17
  220.8 1.0 fusion.18
  221.8 0.0 copy-start.4
  221.8 0.7 fusion.223
  222.6 1.9 collective-permute-start.4
  224.5 2.4 %collective-permute-start.5 = (f32[16,1,256]{2,1,0:T(1,128)S(1)}, f32[16,1,256]{2,1,0:T(1,128)S(1)}, u32[]{:S(2)}, u32[]{:S(2)}) collective-permute-start(f32[16,1,256]{2,1,0:T(1,128)S(1)} %get-tuple-element.10), channel_id=1, source_target_pairs={{4,0},{8,4},{12,8},{16,12},{20,16},{24,20},{28,24},{5,1},{9,5},{13... | collective-permute-start | bytes 49160 | tf_op jit(solution)/shard_map/ppermute | solution.py:17
  226.9 2.6 %collective-permute-done.5 = f32[16,1,256]{2,1,0:T(1,128)S(1)} collective-permute-done((f32[16,1,256]{2,1,0:T(1,128)S(1)}, f32[16,1,256]{2,1,0:T(1,128)S(1)}, u32[]{:S(2)}, u32[]{:S(2)}) %collective-permute-start.5) | collective-permute-done | bytes 16416 | tf_op jit(solution)/shard_map/ppermute | solution.py:17
  229.6 1.0 convolution_bitcast_fusion
  (19 shorter events, 0.1 us)
Async XLA Ops:
  0.6 56.2 %copy-start = (f32[31]{0:T(128)S(1)}, f32[31]{0:T(128)}, u32[]{:S(2)}) copy-start(f32[31]{0:T(128)} %param.15) | copy-start | bytes 376
  0.6 7.9 %copy-start.1 = (f32[31]{0:T(128)S(1)}, f32[31]{0:T(128)}, u32[]{:S(2)}) copy-start(f32[31]{0:T(128)} %param.13) | copy-start | bytes 376
  2.0 12.9 %collective-permute-start = (f32[16,15,512]{2,1,0:T(8,128)S(1)}, f32[16,15,512]{2,1,0:T(8,128)S(1)}, u32[]{:S(2)}, u32[]{:S(2)}) collective-permute-start(f32[16,15,512]{2,1,0:T(8,128)S(1)} %get-tuple-element.7), channel_id=1, source_target_pairs={{0,4},{4,8},{8,12},{12,16},{16,20},{20,24},{24,28},{1,5},{5,9},{9,... | collective-permute-start | bytes 1474568 | tf_op jit(solution)/shard_map/ppermute | solution.py:16
  6.5 13.4 %collective-permute-start.1 = (f32[16,15,512]{2,1,0:T(8,128)S(1)}, f32[16,15,512]{2,1,0:T(8,128)S(1)}, u32[]{:S(2)}, u32[]{:S(2)}) collective-permute-start(f32[16,15,512]{2,1,0:T(8,128)S(1)} %get-tuple-element.8), channel_id=1, source_target_pairs={{4,0},{8,4},{12,8},{16,12},{20,16},{24,20},{28,24},{5,1},{9,5},{13... | collective-permute-start | bytes 1474568 | tf_op jit(solution)/shard_map/ppermute | solution.py:17
  8.6 4.9 %copy-start.5 = (f32[31]{0:T(128)S(1)}, f32[31]{0:T(128)}, u32[]{:S(2)}) copy-start(f32[31]{0:T(128)} %param.14) | copy-start | bytes 376
  8.6 11.3 %copy-start.2 = (f32[16,16,512]{2,1,0:T(8,128)S(1)}, f32[16,16,512]{2,1,0:T(8,128)}, u32[]{:S(2)}) copy-start(f32[16,16,512]{2,1,0:T(8,128)} %param.11) | copy-start | bytes 1572868
  52.1 29.5 %all-to-all-start = ((f32[4,1,32768]{2,1,0:T(1,128)}), f32[4,1,32768]{2,1,0:T(1,128)S(1)}, u32[]{:S(2)}, u32[]{:S(2)}) async-start(f32[4,1,32768]{2,1,0:T(1,128)} %reshape.229), calls=%async_computation | async-start | bytes 1048576 | tf_op jit(solution)/shard_map/all_to_all | solution.py:77
  91.0 6.3 %copy-start.3 = (f32[16,16,512]{2,1,0:T(8,128)S(1)}, f32[16,16,512]{2,1,0:T(8,128)}, u32[]{:S(2)}) copy-start(f32[16,16,512]{2,1,0:T(8,128)} %param.12) | copy-start | bytes 1572868
  92.8 13.7 %all-to-all-start.1 = ((f32[64,16,128]{2,1,0:T(8,128)}), f32[64,16,128]{2,1,0:T(8,128)S(1)}, u32[]{:S(2)}, u32[]{:S(2)}) async-start(f32[64,16,128]{2,1,0:T(8,128)} %copy.22), calls=%async_computation.1 | async-start | bytes 1048576 | tf_op jit(solution)/shard_map/all_to_all | solution.py:80
  119.9 28.4 %all-to-all-start.2 = ((f32[4,1,32768]{2,1,0:T(1,128)}), f32[4,1,32768]{2,1,0:T(1,128)S(1)}, u32[]{:S(2)}, u32[]{:S(2)}) async-start(f32[4,1,32768]{2,1,0:T(1,128)} %reshape.231), calls=%async_computation.2 | async-start | bytes 1048576 | tf_op jit(solution)/shard_map/all_to_all | solution.py:83
  197.0 20.4 %collective-permute-start.2 = (f32[16,15,512]{2,1,0:T(8,128)S(1)}, f32[16,15,512]{2,1,0:T(8,128)S(1)}, u32[]{:S(2)}, u32[]{:S(2)}) collective-permute-start(f32[16,15,512]{2,1,0:T(8,128)S(1)} %get-tuple-element.4), channel_id=1, source_target_pairs={{0,4},{4,8},{8,12},{12,16},{16,20},{20,24},{24,28},{1,5},{5,9},{9,... | collective-permute-start | bytes 1474568 | tf_op jit(solution)/shard_map/ppermute | solution.py:16
  210.3 10.5 %collective-permute-start.3 = (f32[16,15,512]{2,1,0:T(8,128)S(1)}, f32[16,15,512]{2,1,0:T(8,128)S(1)}, u32[]{:S(2)}, u32[]{:S(2)}) collective-permute-start(f32[16,15,512]{2,1,0:T(8,128)S(1)} %get-tuple-element.6), channel_id=1, source_target_pairs={{4,0},{8,4},{12,8},{16,12},{20,16},{24,20},{28,24},{5,1},{9,5},{13... | collective-permute-start | bytes 1474568 | tf_op jit(solution)/shard_map/ppermute | solution.py:17
  221.8 8.8 %copy-start.4 = (f32[16,16,512]{2,1,0:T(8,128)}, f32[16,16,512]{2,1,0:T(8,128)S(1)}, u32[]{:S(2)}) copy-start(f32[16,16,512]{2,1,0:T(8,128)S(1)} %fusion.18) | copy-start | bytes 1572868
  222.6 4.4 %collective-permute-start.4 = (f32[16,1,256]{2,1,0:T(1,128)S(1)}, f32[16,1,256]{2,1,0:T(1,128)S(1)}, u32[]{:S(2)}, u32[]{:S(2)}) collective-permute-start(f32[16,1,256]{2,1,0:T(1,128)S(1)} %get-tuple-element.9), channel_id=1, source_target_pairs={{0,4},{4,8},{8,12},{12,16},{16,20},{20,24},{24,28},{1,5},{5,9},{9,... | collective-permute-start | bytes 49160 | tf_op jit(solution)/shard_map/ppermute | solution.py:16
  224.5 5.1 %collective-permute-start.5 = (f32[16,1,256]{2,1,0:T(1,128)S(1)}, f32[16,1,256]{2,1,0:T(1,128)S(1)}, u32[]{:S(2)}, u32[]{:S(2)}) collective-permute-start(f32[16,1,256]{2,1,0:T(1,128)S(1)} %get-tuple-element.10), channel_id=1, source_target_pairs={{4,0},{8,4},{12,8},{16,12},{20,16},{24,20},{28,24},{5,1},{9,5},{13... | collective-permute-start | bytes 49160 | tf_op jit(solution)/shard_map/ppermute | solution.py:17
where the time goes:
time: 232 us; the launch traced here: 231 us
  local copies, waits for them, and re-layouts  97.8 us (42%)
  matrix products  50.9 us (22%)
  starting transfers between devices  38.8 us (17%)
  waiting for transfers between devices  16.6 us (7%)
  blocking collectives  15.2 us (7%)
  other arithmetic  10.3 us (4%)
    gather x10, local copies, waits for them, and re-layouts, banded(): values = jnp.take(kernel, jnp.clip(offset_index, 0, tap_count - 1))  60.7 us
    dot_general x3, matrix products, across_columns(): return jnp.dot(volume, matrix, precision=PRECISE)  46.6 us
    unnamed x17, local copies, waits for them, and re-layouts  19.8 us
    ppermute x3, starting transfers between devices, extended(): before = lax.ppermute(last, axis, up)  19.7 us
    all_to_all x1, blocking collectives, shards(): lax.all_to_all(turned_back, 'slab', split_axis=0, concat_axis=2, tiled=True)  15.2 us
    ppermute x3, waiting for transfers between devices, extended(): after = lax.ppermute(initial, axis, down)  11 us
    ppermute x3, starting transfers between devices, extended(): after = lax.ppermute(initial, axis, down)  6.46 us
    div x1, other arithmetic, shards(): quotient = observed / blurred  5.99 us
  transfers between devices with their start and end apart: 9, of which 4 were waited for; matrix products, arithmetic and copies ran while one was open for 28% of the time, Pallas kernels for 0%

commit v1 on v0

--- a/solution.py
+++ b/solution.py
@@ -4,6 +4,18 @@
 from jax.sharding import PartitionSpec as P
 
 PRECISE = lax.Precision.HIGHEST
+
+
+def rotated_exchange(x, axis, split, join):
+    ways, here = (lax.axis_size(axis), lax.axis_index(axis))
+    width = x.shape[split] // ways
+    turned = jnp.roll(x, -here * width, axis=split)
+    got = [lax.slice_in_dim(turned, 0, width, axis=split)]
+    for far in range(1, ways):
+        sent = lax.slice_in_dim(turned, far * width, (far + 1) * width, axis=split)
+        got.append(lax.ppermute(sent, axis, [(d, (d + far) % ways) for d in range(ways)]))
+    line = jnp.concatenate(got[::-1], axis=join)
+    return jnp.roll(line, (here + 1) * got[0].shape[join], axis=join)
 
 
 def extended(shard, sides, width):
@@ -73,10 +85,7 @@
     )
     forward_depth = banded(kernel_planes, planes_all, planes_all, 1, reach_cells)
     backward_depth = banded(kernel_planes, planes_all, planes_all, -1, reach_cells)
-    turned = across_depth(
-        lax.all_to_all(partial_value, "slab", split_axis=2, concat_axis=0, tiled=True),
-        forward_depth,
-    )
+    turned = across_depth(rotated_exchange(partial_value, "slab", 2, 0), forward_depth)
     blurred = lax.all_to_all(turned, "slab", split_axis=0, concat_axis=2, tiled=True)
     quotient = observed / blurred
     turned_back = across_depth(

time: 232 us -> 218 us (0.940)
  local copies, waits for them, and re-layouts: 97.8 us -> 83 us
  waiting for transfers between devices: 16.6 us -> 22.5 us
  starting transfers between devices: 38.8 us -> 33.4 us
  blocking collectives: 15.2 us -> 18 us
    unnamed x17 -> x22, local copies, waits for them, and re-layouts: 19.8 us -> 11.8 us
    ppermute x0 -> x3, waiting for transfers between devices: none -> 5.15 us  [rotated_exchange(): lax.ppermute(sent, axis, [(d, (d + far) % ways) for d in range(ways)])]
    all_to_all x1 -> x0, starting transfers between devices: 4.59 us -> none  [shards(): lax.all_to_all(partial_value, 'slab', split_axis=2, concat_axis=0, tiled=...]
    all_to_all x2 -> x0, local copies, waits for them, and re-layouts: 3.84 us -> none  [shards(): lax.all_to_all(partial_value, 'slab', split_axis=2, concat_axis=0, tiled=...]
    ppermute x0 -> x3, starting transfers between devices: none -> 3.81 us  [rotated_exchange(): lax.ppermute(sent, axis, [(d, (d + far) % ways) for d in range(ways)])]
    dot_general x1 -> x0, local copies, waits for them, and re-layouts: 3.64 us -> none  [across_columns(): return jnp.dot(volume, matrix, precision=PRECISE)]
    ppermute x3, starting transfers between devices: 19.7 us -> 16.2 us  [extended(): before = lax.ppermute(last, axis, up)]
    all_to_all x1, blocking collectives: 15.2 us -> 18 us  [shards(): lax.all_to_all(turned_back, 'slab', split_axis=0, concat_axis=2, tiled=True)]
  transfers between devices with their start and end apart: 9 -> 11, of which waited for: 4 -> 5; matrix products, arithmetic and copies ran while one was open for 28% -> 30% of each run, Pallas kernels for 0% -> 0%
where the time goes in v1:
time: 218 us; the launch traced here: 217 us
  local copies, waits for them, and re-layouts  83 us (38%)
  matrix products  51.1 us (23%)
  starting transfers between devices  33.4 us (15%)
  waiting for transfers between devices  22.5 us (10%)
  blocking collectives  18 us (8%)
  other arithmetic  8.39 us (4%)
    gather x10, local copies, waits for them, and re-layouts, banded(): values = jnp.take(kernel, jnp.clip(offset_index, 0, tap_count - 1))  60.7 us
    dot_general x3, matrix products, across_columns(): return jnp.dot(volume, matrix, precision=PRECISE)  46.7 us
    all_to_all x1, blocking collectives, shards(): lax.all_to_all(turned_back, 'slab', split_axis=0, concat_axis=2, tiled=True)  18 us
    ppermute x3, starting transfers between devices, extended(): before = lax.ppermute(last, axis, up)  16.2 us
    unnamed x22, local copies, waits for them, and re-layouts  11.8 us
    ppermute x3, waiting for transfers between devices, extended(): after = lax.ppermute(initial, axis, down)  11 us
    all_to_all x1, waiting for transfers between devices, shards(): lax.all_to_all(turned, 'slab', split_axis=0, concat_axis=2, tiled=True)  6.38 us
    ppermute x3, starting transfers between devices, extended(): after = lax.ppermute(initial, axis, down)  6.24 us
  transfers between devices with their start and end apart: 11, of which 5 were waited for; matrix products, arithmetic and copies ran while one was open for 30% of the time, Pallas kernels for 0%

profile of v1, /device:TPU:1, one launch (start us, length us, event | category | flops | bytes accessed | tf_op | source)
XLA Modules:
  0.0 217.4 jit_solution(7360512395262926035)
XLA Ops:
  0.6 0.0 copy-start
  0.7 1.3 fusion.574
  2.0 4.5 %collective-permute-start = (f32[16,15,512]{2,1,0:T(8,128)S(1)}, f32[16,15,512]{2,1,0:T(8,128)S(1)}, u32[]{:S(2)}, u32[]{:S(2)}) collective-permute-start(f32[16,15,512]{2,1,0:T(8,128)S(1)} %get-tuple-element.10), channel_id=1, source_target_pairs={{0,4},{4,8},{8,12},{12,16},{16,20},{20,24},{24,28},{1,5},{5,9},{9,... | collective-permute-start | bytes 1474568 | tf_op jit(solution)/shard_map/ppermute | solution.py:28
  6.5 1.9 collective-permute-start.1
  8.5 0.1 reshape.143
  8.6 0.1 reshape.155
  8.7 0.0 copy-start.5
  8.7 0.0 copy-start.2
  8.7 4.8 %gather_fusion.3 = f32[736]{0:T(1024)S(1)} fusion(f32[31]{0:T(128)S(1)} %copy-done.1, s32[1024]{0:T(1024)S(1)} %get-tuple-element.47), kind=kCustom, calls=%fused_computation.2.clone | custom fusion | bytes 8832 | tf_op jit(solution)/shard_map/jit(_take)/gather | solution.py:45
  13.5 0.1 reshape.158
  13.6 0.1 reshape.147
  13.7 0.1 reshape.151
  13.8 0.7 fusion.577
  14.5 0.7 fusion.576
  15.2 0.0 collective-permute-done
  15.2 4.7 %collective-permute-done.1 = f32[16,15,512]{2,1,0:T(8,128)S(1)} collective-permute-done((f32[16,15,512]{2,1,0:T(8,128)S(1)}, f32[16,15,512]{2,1,0:T(8,128)S(1)}, u32[]{:S(2)}, u32[]{:S(2)}) %collective-permute-start.1) | collective-permute-done | bytes 491552 | tf_op jit(solution)/shard_map/ppermute | solution.py:29
  19.9 1.0 fusion.15
  20.9 23.0 %fusion.23 = f32[16,16,512]{2,1,0:T(8,128)S(1)} fusion(f32[16,16,512]{2,1,0:T(8,128)S(1)} %fusion.15, f32[]{:T(128)} %bitcast.35, f32[]{:T(128)} %bitcast.34, f32[]{:T(128)} %bitcast.33, f32[]{:T(128)} %bitcast.32, f32[]{:T(128)} %bitcast.31, f32[]{:T(128)} %bitcast.30, f32[]{:T(128)} %bitcast.29, f32[]{:T(128)} %bitcast.28, f32[]{:T(128)} %bitcast.27, ...), kind=kOutput, calls=%fused_computation.27 | convolution fusion | flops 824705024 | bytes 1048700 | tf_op jit(solution)/shard_map/dot_general | solution.py:71
  43.9 0.1 fusion.223
  44.1 3.4 %collective-permute-start.2 = (f32[16,16,128]{2,1,0:T(8,128)S(1)}, f32[16,16,128]{2,1,0:T(8,128)S(1)}, u32[]{:S(2)}, u32[]{:S(2)}) collective-permute-start(f32[16,16,128]{2,1,0:T(8,128)S(1)} %get-tuple-element.9), channel_id=1, source_target_pairs={{0,3},{1,0},{2,1},{3,2},{4,7},{5,4},{6,5},{7,6},{8,11},{9,8},{10,9... | collective-permute-start | bytes 393224 | tf_op jit(solution)/shard_map/ppermute | solution.py:16
  47.5 0.0 collective-permute-start.3
  47.5 24.7 %gather_fusion.2 = f32[4096]{0:T(1024)S(1)} fusion(f32[31]{0:T(128)S(1)} %copy-done, s32[4096]{0:T(1024)S(1)} %get-tuple-element.45), kind=kCustom, calls=%fused_computation.3.clone | custom fusion | bytes 49152 | tf_op jit(solution)/shard_map/jit(_take)/gather | solution.py:45
  72.2 0.1 reshape.154
  72.3 0.4 collective-permute-start.4
  72.7 0.0 collective-permute-done.2
  72.7 0.0 collective-permute-done.3
  72.8 5.1 %collective-permute-done.4 = f32[16,16,128]{2,1,0:T(8,128)S(1)} collective-permute-done((f32[16,16,128]{2,1,0:T(8,128)S(1)}, f32[16,16,128]{2,1,0:T(8,128)S(1)}, u32[]{:S(2)}, u32[]{:S(2)}) %collective-permute-start.4) | collective-permute-done | bytes 131104 | tf_op jit(solution)/shard_map/ppermute | solution.py:16
  78.1 0.0 copy-start.3
  78.1 0.7 fusion.226
  78.8 1.1 copy.21
  79.9 3.5 %all-to-all-start = ((f32[64,16,128]{2,1,0:T(8,128)}), f32[64,16,128]{2,1,0:T(8,128)S(1)}, u32[]{:S(2)}, u32[]{:S(2)}) async-start(f32[64,16,128]{2,1,0:T(8,128)} %copy.21), calls=%async_computation | async-start | bytes 1048576 | tf_op jit(solution)/shard_map/all_to_all | solution.py:89
  83.4 3.7 %copy.23 = f32[16,16,512]{1,0,2:T(8,128)} copy(f32[16,16,512]{2,1,0:T(8,128)S(1)} %copy-done.3) | data formatting | bytes 1048576 | tf_op args[1]
  87.1 6.4 %all-to-all-done = f32[64,16,128]{2,1,0:T(8,128)S(1)} async-done(((f32[64,16,128]{2,1,0:T(8,128)}), f32[64,16,128]{2,1,0:T(8,128)S(1)}, u32[]{:S(2)}, u32[]{:S(2)}) %all-to-all-start) | async-done | bytes 524320 | tf_op jit(solution)/shard_map/all_to_all | solution.py:89
  93.5 2.8 %copy.22 = f32[16,16,4,128]{1,0,3,2:T(8,128)} copy(f32[16,16,4,128]{3,1,0,2:T(8,128)S(1)} %bitcast.115) | data formatting | bytes 1048576 | tf_op jit(solution)/shard_map/all_to_all | solution.py:89
  96.3 6.0 %bitcast_divide_fusion = f32[16,16,512]{1,0,2:T(8,128)} fusion(f32[16,16,512]{1,0,2:T(8,128)} %copy.23, f32[16,16,4,128]{1,0,3,2:T(8,128)} %copy.22), kind=kLoop, calls=%fused_computation.4 | loop fusion | flops 131072 | bytes 1572864 | tf_op jit(solution)/shard_map/div | solution.py:90
  102.3 4.6 %reshape.229 = f32[4,1,32768]{2,1,0:T(1,128)} reshape(f32[512,16,16]{2,1,0:T(8,128)} %bitcast.113) | data formatting | bytes 1048576
  106.9 3.7 %all-to-all-start.1 = ((f32[4,1,32768]{2,1,0:T(1,128)}), f32[4,1,32768]{2,1,0:T(1,128)S(1)}, u32[]{:S(2)}, u32[]{:S(2)}) async-start(f32[4,1,32768]{2,1,0:T(1,128)} %reshape.229), calls=%async_computation.1 | async-start | bytes 1048576 | tf_op jit(solution)/shard_map/all_to_all | solution.py:92
  110.6 24.7 %gather_fusion.1 = f32[4096]{0:T(1024)S(1)} fusion(f32[31]{0:T(128)S(1)} %copy-done, s32[4096]{0:T(1024)S(1)} %get-tuple-element.46), kind=kCustom, calls=%fused_computation.1.clone | custom fusion | bytes 49152 | tf_op jit(solution)/shard_map/jit(_take)/gather | solution.py:45
  135.3 0.1 reshape.150
  135.4 0.5 broadcast.950
  135.9 2.2 reduce
  138.1 3.4 %reshape.230 = f32[512,16,16]{2,1,0:T(8,128)} reshape(f32[4,32768]{1,0:T(4,128)S(1)} %reduce) | data formatting | bytes 1048576
  141.5 3.3 %copy.24 = f32[16,16,4,128]{3,0,2,1:T(8,128)S(1)} copy(f32[16,16,4,128]{1,0,3,2:T(8,128)} %bitcast.114) | data formatting | bytes 1048576 | tf_op jit(solution)/shard_map/all_to_all | solution.py:92
  144.8 0.6 fusion.383
  145.5 0.3 copy.26
  145.8 18.0 %all_to_all.54 = f32[64,16,128]{2,1,0:T(8,128)S(1)} all-to-all(f32[64,16,128]{2,1,0:T(8,128)S(1)} %copy.26), channel_id=1, replica_groups=mesh['tile'=8,'slab'=4] {'slab'}, dimensions={0} | all-to-all | bytes 1048576 | tf_op jit(solution)/shard_map/all_to_all | solution.py:94
  163.7 0.3 copy.40
  164.1 0.2 all_to_all.50
  164.3 23.0 %fusion.21 = f32[16,16,512]{2,1,0:T(8,128)S(1)} fusion(f32[16,16,512]{2,1,0:T(8,128)S(1)} %all_to_all.50, f32[]{:T(128)} %bitcast.35, f32[]{:T(128)} %bitcast.34, f32[]{:T(128)} %bitcast.33, f32[]{:T(128)} %bitcast.32, f32[]{:T(128)} %bitcast.31, f32[]{:T(128)} %bitcast.30, f32[]{:T(128)} %bitcast.29, f32[]{:T(128)} %bitcast.28, f32[]{:T(128)} %bitcast.27, ...), kind=kOutput, calls=%fused_computation.25 | convolution fusion | flops 824967168 | bytes 1048700 | tf_op jit(solution)/shard_map/dot_general | solution.py:71
  187.3 0.1 fusion.572
  187.4 9.8 %collective-permute-start.5 = (f32[16,15,512]{2,1,0:T(8,128)S(1)}, f32[16,15,512]{2,1,0:T(8,128)S(1)}, u32[]{:S(2)}, u32[]{:S(2)}) collective-permute-start(f32[16,15,512]{2,1,0:T(8,128)S(1)} %get-tuple-element.4), channel_id=1, source_target_pairs={{0,4},{4,8},{8,12},{12,16},{16,20},{20,24},{24,28},{1,5},{5,9},{9,... | collective-permute-start | bytes 1474568 | tf_op jit(solution)/shard_map/ppermute | solution.py:28
  197.1 1.9 collective-permute-start.6
  199.1 4.8 %gather_fusion = f32[736]{0:T(1024)S(1)} fusion(f32[31]{0:T(128)S(1)} %copy-done.1, s32[1024]{0:T(1024)S(1)} %get-tuple-element.48), kind=kCustom, calls=%fused_computation.clone | custom fusion | bytes 8832 | tf_op jit(solution)/shard_map/jit(_take)/gather | solution.py:45
  203.9 0.1 reshape.146
  203.9 0.0 collective-permute-done.5
  204.0 3.7 %collective-permute-done.6 = f32[16,15,512]{2,1,0:T(8,128)S(1)} collective-permute-done((f32[16,15,512]{2,1,0:T(8,128)S(1)}, f32[16,15,512]{2,1,0:T(8,128)S(1)}, u32[]{:S(2)}, u32[]{:S(2)}) %collective-permute-start.6) | collective-permute-done | bytes 491552 | tf_op jit(solution)/shard_map/ppermute | solution.py:29
  207.6 1.0 fusion.18
  208.7 0.0 copy-start.4
  208.7 0.7 fusion.224
  209.4 1.9 collective-permute-start.7
  211.4 2.4 %collective-permute-start.8 = (f32[16,1,256]{2,1,0:T(1,128)S(1)}, f32[16,1,256]{2,1,0:T(1,128)S(1)}, u32[]{:S(2)}, u32[]{:S(2)}) collective-permute-start(f32[16,1,256]{2,1,0:T(1,128)S(1)} %get-tuple-element.13), channel_id=1, source_target_pairs={{4,0},{8,4},{12,8},{16,12},{20,16},{24,20},{28,24},{5,1},{9,5},{13... | collective-permute-start | bytes 49160 | tf_op jit(solution)/shard_map/ppermute | solution.py:29
  213.8 0.0 collective-permute-done.7
  213.8 2.6 %collective-permute-done.8 = f32[16,1,256]{2,1,0:T(1,128)S(1)} collective-permute-done((f32[16,1,256]{2,1,0:T(1,128)S(1)}, f32[16,1,256]{2,1,0:T(1,128)S(1)}, u32[]{:S(2)}, u32[]{:S(2)}) %collective-permute-start.8) | collective-permute-done | bytes 16416 | tf_op jit(solution)/shard_map/ppermute | solution.py:29
  216.4 1.0 convolution_bitcast_fusion
  (27 shorter events, 0.3 us)
Async XLA Ops:
  0.6 46.9 %copy-start = (f32[31]{0:T(128)S(1)}, f32[31]{0:T(128)}, u32[]{:S(2)}) copy-start(f32[31]{0:T(128)} %param.15) | copy-start | bytes 376
  0.6 8.0 %copy-start.1 = (f32[31]{0:T(128)S(1)}, f32[31]{0:T(128)}, u32[]{:S(2)}) copy-start(f32[31]{0:T(128)} %param.13) | copy-start | bytes 376
  2.0 13.2 %collective-permute-start = (f32[16,15,512]{2,1,0:T(8,128)S(1)}, f32[16,15,512]{2,1,0:T(8,128)S(1)}, u32[]{:S(2)}, u32[]{:S(2)}) collective-permute-start(f32[16,15,512]{2,1,0:T(8,128)S(1)} %get-tuple-element.10), channel_id=1, source_target_pairs={{0,4},{4,8},{8,12},{12,16},{16,20},{20,24},{24,28},{1,5},{5,9},{9,... | collective-permute-start | bytes 1474568 | tf_op jit(solution)/shard_map/ppermute | solution.py:28
  6.5 13.4 %collective-permute-start.1 = (f32[16,15,512]{2,1,0:T(8,128)S(1)}, f32[16,15,512]{2,1,0:T(8,128)S(1)}, u32[]{:S(2)}, u32[]{:S(2)}) collective-permute-start(f32[16,15,512]{2,1,0:T(8,128)S(1)} %get-tuple-element.11), channel_id=1, source_target_pairs={{4,0},{8,4},{12,8},{16,12},{20,16},{24,20},{28,24},{5,1},{9,5},{13... | collective-permute-start | bytes 1474568 | tf_op jit(solution)/shard_map/ppermute | solution.py:29
  8.7 5.1 %copy-start.5 = (f32[31]{0:T(128)S(1)}, f32[31]{0:T(128)}, u32[]{:S(2)}) copy-start(f32[31]{0:T(128)} %param.14) | copy-start | bytes 376
  8.7 11.2 %copy-start.2 = (f32[16,16,512]{2,1,0:T(8,128)S(1)}, f32[16,16,512]{2,1,0:T(8,128)}, u32[]{:S(2)}) copy-start(f32[16,16,512]{2,1,0:T(8,128)} %param.11) | copy-start | bytes 1572868
  44.1 28.6 %collective-permute-start.2 = (f32[16,16,128]{2,1,0:T(8,128)S(1)}, f32[16,16,128]{2,1,0:T(8,128)S(1)}, u32[]{:S(2)}, u32[]{:S(2)}) collective-permute-start(f32[16,16,128]{2,1,0:T(8,128)S(1)} %get-tuple-element.9), channel_id=1, source_target_pairs={{0,3},{1,0},{2,1},{3,2},{4,7},{5,4},{6,5},{7,6},{8,11},{9,8},{10,9... | collective-permute-start | bytes 393224 | tf_op jit(solution)/shard_map/ppermute | solution.py:16
  47.5 25.3 %collective-permute-start.3 = (f32[16,16,128]{2,1,0:T(8,128)S(1)}, f32[16,16,128]{2,1,0:T(8,128)S(1)}, u32[]{:S(2)}, u32[]{:S(2)}) collective-permute-start(f32[16,16,128]{2,1,0:T(8,128)S(1)} %get-tuple-element.8), channel_id=1, source_target_pairs={{0,2},{1,3},{2,0},{3,1},{4,6},{5,7},{6,4},{7,5},{8,10},{9,11},{10,... | collective-permute-start | bytes 393224 | tf_op jit(solution)/shard_map/ppermute | solution.py:16
  72.3 5.6 %collective-permute-start.4 = (f32[16,16,128]{2,1,0:T(8,128)S(1)}, f32[16,16,128]{2,1,0:T(8,128)S(1)}, u32[]{:S(2)}, u32[]{:S(2)}) collective-permute-start(f32[16,16,128]{2,1,0:T(8,128)S(1)} %get-tuple-element.7), channel_id=1, source_target_pairs={{0,1},{1,2},{2,3},{3,0},{4,5},{5,6},{6,7},{7,4},{8,9},{9,10},{10,1... | collective-permute-start | bytes 393224 | tf_op jit(solution)/shard_map/ppermute | solution.py:16
  78.1 5.3 %copy-start.3 = (f32[16,16,512]{2,1,0:T(8,128)S(1)}, f32[16,16,512]{2,1,0:T(8,128)}, u32[]{:S(2)}) copy-start(f32[16,16,512]{2,1,0:T(8,128)} %param.12) | copy-start | bytes 1572868
  79.9 13.6 %all-to-all-start = ((f32[64,16,128]{2,1,0:T(8,128)}), f32[64,16,128]{2,1,0:T(8,128)S(1)}, u32[]{:S(2)}, u32[]{:S(2)}) async-start(f32[64,16,128]{2,1,0:T(8,128)} %copy.21), calls=%async_computation | async-start | bytes 1048576 | tf_op jit(solution)/shard_map/all_to_all | solution.py:89
  106.9 28.4 %all-to-all-start.1 = ((f32[4,1,32768]{2,1,0:T(1,128)}), f32[4,1,32768]{2,1,0:T(1,128)S(1)}, u32[]{:S(2)}, u32[]{:S(2)}) async-start(f32[4,1,32768]{2,1,0:T(1,128)} %reshape.229), calls=%async_computation.1 | async-start | bytes 1048576 | tf_op jit(solution)/shard_map/all_to_all | solution.py:92
  187.4 16.6 %collective-permute-start.5 = (f32[16,15,512]{2,1,0:T(8,128)S(1)}, f32[16,15,512]{2,1,0:T(8,128)S(1)}, u32[]{:S(2)}, u32[]{:S(2)}) collective-permute-start(f32[16,15,512]{2,1,0:T(8,128)S(1)} %get-tuple-element.4), channel_id=1, source_target_pairs={{0,4},{4,8},{8,12},{12,16},{16,20},{20,24},{24,28},{1,5},{5,9},{9,... | collective-permute-start | bytes 1474568 | tf_op jit(solution)/shard_map/ppermute | solution.py:28
  197.1 10.5 %collective-permute-start.6 = (f32[16,15,512]{2,1,0:T(8,128)S(1)}, f32[16,15,512]{2,1,0:T(8,128)S(1)}, u32[]{:S(2)}, u32[]{:S(2)}) collective-permute-start(f32[16,15,512]{2,1,0:T(8,128)S(1)} %get-tuple-element.6), channel_id=1, source_target_pairs={{4,0},{8,4},{12,8},{16,12},{20,16},{24,20},{28,24},{5,1},{9,5},{13... | collective-permute-start | bytes 1474568 | tf_op jit(solution)/shard_map/ppermute | solution.py:29
  208.7 8.8 %copy-start.4 = (f32[16,16,512]{2,1,0:T(8,128)}, f32[16,16,512]{2,1,0:T(8,128)S(1)}, u32[]{:S(2)}) copy-start(f32[16,16,512]{2,1,0:T(8,128)S(1)} %fusion.18) | copy-start | bytes 1572868
  209.4 4.4 %collective-permute-start.7 = (f32[16,1,256]{2,1,0:T(1,128)S(1)}, f32[16,1,256]{2,1,0:T(1,128)S(1)}, u32[]{:S(2)}, u32[]{:S(2)}) collective-permute-start(f32[16,1,256]{2,1,0:T(1,128)S(1)} %get-tuple-element.12), channel_id=1, source_target_pairs={{0,4},{4,8},{8,12},{12,16},{16,20},{20,24},{24,28},{1,5},{5,9},{9,... | collective-permute-start | bytes 49160 | tf_op jit(solution)/shard_map/ppermute | solution.py:28
  211.4 5.1 %collective-permute-start.8 = (f32[16,1,256]{2,1,0:T(1,128)S(1)}, f32[16,1,256]{2,1,0:T(1,128)S(1)}, u32[]{:S(2)}, u32[]{:S(2)}) collective-permute-start(f32[16,1,256]{2,1,0:T(1,128)S(1)} %get-tuple-element.13), channel_id=1, source_target_pairs={{4,0},{8,4},{12,8},{16,12},{20,16},{24,20},{28,24},{5,1},{9,5},{13... | collective-permute-start | bytes 49160 | tf_op jit(solution)/shard_map/ppermute | solution.py:29
